TPU v7x, 256 devices: a whole 4x4x8 slice. The times are simulated.
256 devices in a mesh: dp: 32 (over z_lo, y, core), graph: 8 (over z_hi, x).
Axes of the slice: x: 4, y: 4, z: 8 (z_hi: 2, z_lo: 4; z = z_hi * 4 + z_lo), core: 2. Of those that a mesh axis runs over, the one named last changes fastest.
Arguments:
- embedding: bfloat16 [32, 12288, 512], P('dp', 'graph'), may hold values from -6 to 6
- triplet_basis: bfloat16 [32, 49152, 64], P('dp', 'graph'), may hold values from -6 to 6
- atom_cotangent: bfloat16 [32, 768, 1024], P('dp', 'graph'), may hold values from -6 to 6
- fidelity: int32 [32, 768], P('dp', 'graph'), may hold values 0 or 1
- edge_target: int32 [32, 12288], P('dp', 'graph'), may hold values from 0 to 767, as said below
- triplet_source: int32 [32, 49152], P('dp', 'graph'), may hold values from 0 to 12287, as said below
- triplet_target: int32 [32, 49152], P('dp', 'graph'), may hold values from 0 to 12287, as said below
- edge_count: int32 [32, 8], P('dp', 'graph'), may hold values from 768 to 1536, as said below
- triplet_count: int32 [32, 8], P('dp', 'graph'), may hold values from 1536 to 6144, as said below
- w_down: bfloat16 [512, 64], replicated, may hold values from -0.25 to 0.25
- w_up: bfloat16 [64, 512], replicated, may hold values from -0.75 to 0.75
- w_atom: bfloat16 [512, 1024], replicated, may hold values from -0.25 to 0.25
Outputs:
- embedding_grad: bfloat16 [32, 12288, 512], P('dp', 'graph')
- w_atom_grad: float32 [512, 1024], P(None, 'graph')
- w_up_grad: float32 [64, 512], replicated
- w_down_grad: float32 [512, 64], replicated
Inputs may be any that keep to these rules, and one draw needn't show every extreme that they name: `edge_target`: edges of index g of graph, slots g * 1536 to (g + 1) * 1536 - 1, have target atoms anywhere in their batch. `triplet_source`: A live edge slot of any index of graph in the same batch. `triplet_target`: A live edge slot of the same index of graph as the triplet slot. `edge_count`: some index of graph of every batch has all 1536 edge slots live. `triplet_count`: some index of graph of every batch has all 6144 triplet slots live.
All inputs are finite; a program needn't handle non-finite values. No bound on the sum of `fidelity` on one device may be relied on, other than what follows from the above.
Results may differ from a plain program's by a relative error of at most 0.0077.
Values may be sent and summed in bfloat16 or wider, within the bound.
No kernel may reach another device: no remote copies, remote signals or barrier semaphores. Data moves between devices by JAX's collectives and lax.ppermute only.
A program may use at most 128 MiB of HBM per device.

v0:
```python
import jax
import jax.numpy as jnp
from jax import lax
from jax.sharding import PartitionSpec as P


def local(
    embedding,
    triplet_basis,
    atom_cotangent,
    fidelity,
    edge_target,
    triplet_source,
    triplet_target,
    edge_count,
    triplet_count,
    w_down,
    w_up,
    w_atom,
):
    rows = embedding[0]
    basis = triplet_basis[0]
    edge_slots = rows.shape[0]
    trip_slots = basis.shape[0]
    groups = lax.axis_size("graph")
    here = lax.axis_index("graph")
    edge_live = jnp.arange(edge_slots, dtype=jnp.int32) < edge_count[0, 0]
    trip_live = jnp.arange(trip_slots, dtype=jnp.int32) < triplet_count[0, 0]
    weight = 1.0 + 3.0 * fidelity[0].astype(jnp.float32)
    scaled = (weight[:, None] * atom_cotangent[0].astype(jnp.float32)).astype(jnp.bfloat16)
    atoms_all = lax.all_gather(scaled, "graph", axis=0, tiled=True)
    projected = jnp.dot(rows, w_down, preferred_element_type=jnp.float32).astype(jnp.bfloat16)
    table = lax.all_gather(projected, "graph", axis=0, tiled=True)
    feats = jnp.take(table, triplet_source[0], axis=0)
    local_dest = triplet_target[0] - here * edge_slots
    product = jnp.where(
        trip_live[:, None], feats.astype(jnp.float32) * basis.astype(jnp.float32), jnp.float32(0.0)
    )
    aggregate = jax.ops.segment_sum(product, local_dest, num_segments=edge_slots).astype(
        jnp.bfloat16
    )
    pre = jnp.dot(aggregate, w_up, preferred_element_type=jnp.float32)
    sig = jax.nn.sigmoid(pre)
    updated = (rows.astype(jnp.float32) + pre * sig).astype(jnp.bfloat16)
    edge_in = jnp.where(
        edge_live[:, None], jnp.take(atoms_all, edge_target[0], axis=0), jnp.zeros((), jnp.bfloat16)
    )
    edge_out = jnp.dot(edge_in, w_atom.T, preferred_element_type=jnp.float32)
    part_atom = jnp.dot(updated.T, edge_in, preferred_element_type=jnp.float32)
    pre_grad = (edge_out * sig * (1.0 + pre * (1.0 - sig))).astype(jnp.bfloat16)
    part_up = jnp.dot(aggregate.T, pre_grad, preferred_element_type=jnp.float32)
    aggregate_grad = jnp.dot(pre_grad, w_up.T, preferred_element_type=jnp.float32).astype(
        jnp.bfloat16
    )
    contrib = jnp.where(
        trip_live[:, None],
        jnp.take(aggregate_grad, local_dest, axis=0).astype(jnp.float32)
        * basis.astype(jnp.float32),
        jnp.float32(0.0),
    )
    partial_grad = jax.ops.segment_sum(
        contrib, triplet_source[0], num_segments=edge_slots * groups
    ).astype(jnp.bfloat16)
    source_grad = (
        lax.psum_scatter(partial_grad, "graph", scatter_dimension=0, tiled=True)
        .astype(jnp.float32)
        .astype(jnp.bfloat16)
    )
    part_down = jnp.dot(rows.T, source_grad, preferred_element_type=jnp.float32)
    result = (edge_out + jnp.dot(source_grad, w_down.T, preferred_element_type=jnp.float32)).astype(
        jnp.bfloat16
    )
    total_atom, up_grad, down_grad = lax.psum((part_atom, part_up, part_down), ("dp", "graph"))
    width = total_atom.shape[1] // groups
    atom_grad = lax.dynamic_slice_in_dim(total_atom, here * width, width, 1)
    return (result[None], atom_grad, up_grad, down_grad)


def solution(mesh):
    return jax.shard_map(
        local,
        mesh=mesh,
        in_specs=(
            P("dp", "graph", None),
            P("dp", "graph", None),
            P("dp", "graph", None),
            P("dp", "graph"),
            P("dp", "graph"),
            P("dp", "graph"),
            P("dp", "graph"),
            P("dp", "graph"),
            P("dp", "graph"),
            P(),
            P(),
            P(),
        ),
        out_specs=(P("dp", "graph", None), P(None, "graph"), P(), P()),
        check_vma=False,
    )
```

profile of v0, /device:TPU:5, one launch (start us, length us, event | category | flops | bytes accessed | tf_op | source)
XLA Modules:
  0.0 700.4 jit_solution(8970966009916328786)
XLA Ops:
  7.2 0.0 copy-start
  7.2 0.0 copy-start.4
  7.2 0.0 copy-start.6
  7.2 0.0 all-gather.3.cloned.1.call-start
  7.2 0.8 add_bitcast_fusion
  8.0 1.7 fusion.30
  9.7 0.0 all-gather.3.cloned.1.call-update
  9.8 0.0 all-gather.5.cloned.1.call-start
  9.8 2.7 convolution_convert_fusion.1
  12.5 0.0 all-gather.5.cloned.1.call-update
  12.5 0.0 reduce-scatter.2.cloned.1.call-start
  13.2 0.8 compare_select_fusion
  14.0 0.7 reduce
  14.7 0.6 iota_compare_fusion.1
  15.3 0.7 fusion.36
  16.7 0.0 copy-done.4
  16.7 0.9 copy.30
  17.6 0.0 copy-done.6
  17.7 0.0 copy-start.8
  17.7 0.0 copy-start.9
  17.7 61.5 %all-gather.3.cloned.1.call-done = bf16[768,1024]{1,0:T(8,128)(2,1)} async-done(((bf16[96,1024]{1,0:T(8,128)(2,1)}), bf16[768,1024]{1,0:T(8,128)(2,1)}) %all-gather.3.cloned.1.call-update) | async-done | bytes 1572880 | tf_op jit(solution)/shard_map/all_gather | solution.py:31
  79.2 9.4 %gather_fusion = bf16[1536,1024]{1,0:T(8,128)(2,1)} fusion(bf16[768,1024]{1,0:T(8,128)(2,1)} %all-gather.3.cloned.1.call-done, s32[2048]{0:T(1024)S(1)} %pad_clamp_fusion), kind=kCustom, calls=%fused_computation | custom fusion | bytes 6297600 | tf_op jit(solution)/shard_map/jit(_take)/gather | solution.py:46
  88.6 0.0 copy-done
  88.6 0.0 copy-done.8
  88.6 0.0 copy-done.9
  88.7 5.5 fusion.40
  94.1 53.0 %all-gather.5.cloned.1.call-done = bf16[12288,64]{0,1:T(8,128)(2,1)} async-done(((bf16[1536,64]{0,1:T(8,128)(2,1)}), bf16[12288,64]{0,1:T(8,128)(2,1)}) %all-gather.5.cloned.1.call-update) | async-done | bytes 1572880 | tf_op jit(solution)/shard_map/all_gather | solution.py:33
  147.1 4.1 copy.29
  151.2 75.0 %scatter_custom_fusion = f32[1536,64]{1,0:T(8,128)S(1)} fusion(s32[6144]{0:T(1024)S(1)} %bitcast.56, bf16[1,6144,64]{2,1,0:T(8,128)(2,1)S(1)} %copy.30, f32[]{:T(128)} %constant.38.clone.1, pred[6144]{0:T(1024)(128)(4,1)S(1)} %get-tuple-element.14, pred[6144]{0:T(1024)(128)(4,1)S(1)} %get-tuple-element.13, bf16[]{:T(256)} %constant.30.clone.1, ...), kind=kCustom, calls=%fused_computation.9 | custom fusion | flops 2359296 | bytes 5150208 | tf_op jit(solution)/shard_map/scatter-add | solution.py:39
  226.2 0.0 copy-start.7
  226.2 5.0 multiply_convert_fusion
  231.2 0.0 copy-start.2
  231.2 1.1 copy-done.2
  232.4 0.0 copy-done.7
  232.4 1.3 convolution_convert_fusion
  233.6 1.8 copy.31
  235.5 77.6 %scatter_custom_fusion.1 = f32[12288,64]{1,0:T(8,128)} fusion(s32[6144]{0:T(1024)S(1)} %bitcast.52, f32[]{:T(128)} %constant.38.clone.1, bf16[1,6144,64]{2,1,0:T(8,128)(2,1)S(1)} %copy.30, pred[6144]{0:T(1024)(128)(4,1)S(1)} %compare_and_fusion.1, pred[6144]{0:T(1024)(128)(4,1)S(1)} %get-tuple-element.13, bf16[]{:T(256)} %constant.30.clone.1, ...), kind=kCustom, calls=%fused_computation.11 | custom fusion | flops 2359296 | bytes 5150208 | tf_op jit(solution)/shard_map/scatter-add | solution.py:61
  313.1 4.2 convert_element_type.68
  317.2 0.0 copy-start.1
  317.2 0.0 reduce-scatter.2.cloned.1.call-update
  317.3 0.0 all-reduce.3.cloned.1.call-start
  317.3 2.6 fusion.32
  319.9 0.0 copy-done.1
  319.9 6.4 fusion.20
  326.3 0.0 copy-start.5
  326.3 94.9 %reduce-scatter.2.cloned.1.call-done = bf16[1536,64]{1,0:T(8,128)(2,1)} async-done(((bf16[12288,64]{1,0:T(8,128)(2,1)}), bf16[1536,64]{1,0:T(8,128)(2,1)}) %reduce-scatter.2.cloned.1.call-update) | async-done | bytes 196624 | tf_op jit(solution)/shard_map/reduce_scatter | solution.py:65
  421.2 0.0 copy-start.3
  421.2 2.1 fusion.25
  423.3 0.0 all-reduce.3.cloned.1.call-update
  423.4 0.0 copy-done.5
  423.4 0.0 copy-done.3
  423.4 3.6 fusion.10
  427.0 262.0 %all-reduce.3.cloned.1.call-done = (f32[512,1024]{1,0:T(8,128)}, f32[64,512]{1,0:T(8,128)}, f32[512,64]{0,1:T(8,128)}) async-done(((f32[512,1024]{1,0:T(8,128)}, f32[64,512]{1,0:T(8,128)}, f32[512,64]{0,1:T(8,128)}), (f32[512,1024]{1,0:T(8,128)}, f32[64,512]{1,0:T(8,128)}, f32[512,64]{0,1:T(8,128)})) %all-reduce.3.cloned.1.call-update) | async-done | bytes 2359312 | tf_op jit(solution)/shard_map/psum | solution.py:73
  689.0 1.7 constant_dynamic-slice_fusion
  690.7 1.6 copy.37
  692.3 1.6 copy.38
  (6 shorter events, 0.1 us)
Async XLA Ops:
  7.2 81.5 %copy-start = (bf16[512,1024]{1,0:T(8,128)(2,1)S(1)}, bf16[512,1024]{1,0:T(8,128)(2,1)}, u32[]{:S(2)}) copy-start(bf16[512,1024]{1,0:T(8,128)(2,1)} %param.23) | copy-start | bytes 3145732
  7.2 9.5 %copy-start.4 = (bf16[1,6144,64]{1,2,0:T(8,128)(2,1)S(1)}, bf16[1,6144,64]{1,2,0:T(8,128)(2,1)}, u32[]{:S(2)}) copy-start(bf16[1,6144,64]{1,2,0:T(8,128)(2,1)} %param.13) | copy-start | bytes 2359300
  7.2 10.4 %copy-start.6 = (s32[1,6144]{1,0:T(1,128)S(1)}, s32[1,6144]{1,0:T(1,128)}, u32[]{:S(2)}) copy-start(s32[1,6144]{1,0:T(1,128)} %param.17) | copy-start | bytes 73732
  7.2 72.0 %all-gather.3.cloned.1.call-start = ((), (), s32[]{:S(2)}) async-start(), calls=%async_computation.1 | async-start | bytes 1769472 | tf_op jit(solution)/shard_map/all_gather | solution.py:31
  9.8 137.3 %all-gather.5.cloned.1.call-start = ((), (), s32[]{:S(2)}) async-start(), calls=%async_computation.2 | async-start | bytes 1769472 | tf_op jit(solution)/shard_map/all_gather | solution.py:33
  12.5 408.7 %reduce-scatter.2.cloned.1.call-start = ((), (), s32[]{:S(2)}) async-start(), calls=%async_computation.3 | async-start | bytes 3538944 | tf_op jit(solution)/shard_map/reduce_scatter | solution.py:65
  17.7 71.0 %copy-start.8 = (pred[1536]{0:T(1024)(128)(4,1)S(1)}, pred[1536]{0:T(1024)(128)(4,1)}, u32[]{:S(2)}) copy-start(pred[1536]{0:T(1024)(128)(4,1)} %get-tuple-element.11) | copy-start | bytes 4612
  17.7 71.0 %copy-start.9 = (pred[1536]{0:T(1024)(128)(4,1)S(1)}, pred[1536]{0:T(1024)(128)(4,1)}, u32[]{:S(2)}) copy-start(pred[1536]{0:T(1024)(128)(4,1)} %get-tuple-element.12) | copy-start | bytes 4612
  226.2 6.2 copy-start.7
  231.2 1.1 copy-start.2
  317.2 2.7 copy-start.1
  317.3 371.8 %all-reduce.3.cloned.1.call-start = ((), (), s32[]{:S(2)}) async-start(), calls=%async_computation.4 | async-start | bytes 4718592 | tf_op jit(solution)/shard_map/psum | solution.py:73
  326.3 97.1 %copy-start.5 = (bf16[512,64]{0,1:T(8,128)(2,1)S(1)}, bf16[512,64]{0,1:T(8,128)(2,1)}, u32[]{:S(2)}) copy-start(bf16[512,64]{0,1:T(8,128)(2,1)} %param.21) | copy-start | bytes 196612
  421.2 2.2 copy-start.3
Sparse Core Ops, SparseCore 0:
  11.2 68.0 all-gather.2
  82.4 64.6 all-gather.4
  317.4 103.7 reduce-scatter.1
  427.3 261.6 all-reduce.2
where the time goes:
time: 703 us; the launch traced here: 700 us
  waiting for transfers between devices  472 us (67%)
  other arithmetic  162 us (23%)
  matrix products  29.2 us (4%)
  local copies, waits for them, and re-layouts  22.2 us (3%)
  between operations  15.2 us (2%)
    psum x1, waiting for transfers between devices, local(): lax.psum((part_atom, part_up, part_down), ('dp', 'graph'))  262 us
    reduce_scatter x1, waiting for transfers between devices, local(): lax.psum_scatter(partial_grad, 'graph', scatter_dimension=0, tiled=True)  94.9 us
    scatter-add x1, other arithmetic, local(): jax.ops.segment_sum(contrib, triplet_source[0], num_segments=edge_slots *...  77.6 us
    scatter-add x1, other arithmetic, local(): jax.ops.segment_sum(product, local_dest, num_segments=edge_slots)  75 us
    all_gather x1, waiting for transfers between devices, local(): atoms_all = lax.all_gather(scaled, 'graph', axis=0, tiled=True)  61.5 us
    all_gather x1, waiting for transfers between devices, local(): table = lax.all_gather(projected, 'graph', axis=0, tiled=True)  53 us
  transfers between devices with their start and end apart: 4, of which 4 were waited for; matrix products, arithmetic and copies ran while one was open for 5% of the time, Pallas kernels for 0%

commit v1 on v0

v1 whole, which is shorter than its diff:
```python
import jax
import jax.numpy as jnp
from jax import lax
from jax.sharding import PartitionSpec as P


def shifted(x, axis, size, k):
    return lax.ppermute(x, axis, [(i, (i + k) % size) for i in range(size)])


def butterfly(x, axis, size):
    bit = 1
    while bit < size:
        x = x + lax.ppermute(x, axis, [(i, i ^ bit) for i in range(size)])
        bit *= 2
    return x


def local(
    embedding,
    triplet_basis,
    atom_cotangent,
    fidelity,
    edge_target,
    triplet_source,
    triplet_target,
    edge_count,
    triplet_count,
    w_down,
    w_up,
    w_atom,
):
    rows = embedding[0]
    basis = triplet_basis[0]
    edge_slots, de = rows.shape
    trip_slots, db = basis.shape
    atom_slots, da = atom_cotangent.shape[1:]
    groups = lax.axis_size("graph")
    dps = lax.axis_size("dp")
    here = lax.axis_index("graph")
    edge_live = jnp.arange(edge_slots, dtype=jnp.int32) < edge_count[0, 0]
    trip_live = jnp.arange(trip_slots, dtype=jnp.int32) < triplet_count[0, 0]
    weight = 1.0 + 3.0 * fidelity[0].astype(jnp.float32)
    scaled = (weight[:, None] * atom_cotangent[0].astype(jnp.float32)).astype(jnp.bfloat16)
    projected = jnp.dot(rows, w_down, preferred_element_type=jnp.float32).astype(jnp.bfloat16)

    packed = jnp.concatenate([scaled.reshape(-1), projected.reshape(-1)])
    pieces = [packed] + [shifted(packed, "graph", groups, k) for k in range(1, groups)]
    got = jnp.stack(pieces)
    n_atom = atom_slots * da
    atoms_all = got[:, :n_atom].reshape(groups * atom_slots, da)
    table = got[:, n_atom:].reshape(groups * edge_slots, db)

    source = triplet_source[0]
    src_row = ((here - source // edge_slots) % groups) * edge_slots + source % edge_slots
    feats = jnp.take(table, src_row, axis=0)
    target = edge_target[0]
    tgt_row = ((here - target // atom_slots) % groups) * atom_slots + target % atom_slots

    local_dest = triplet_target[0] - here * edge_slots
    product = feats.astype(jnp.float32) * basis.astype(jnp.float32)
    hi = product.astype(jnp.bfloat16)
    lo = (product - hi.astype(jnp.float32)).astype(jnp.bfloat16)
    pick = (local_dest[None, :] == jnp.arange(edge_slots, dtype=jnp.int32)[:, None]) & trip_live[None, :]
    summed = jnp.dot(
        pick.astype(jnp.bfloat16),
        jnp.concatenate([hi, lo], axis=1),
        preferred_element_type=jnp.float32,
    )
    aggregate = (summed[:, :db] + summed[:, db:]).astype(jnp.bfloat16)

    pre = jnp.dot(aggregate, w_up, preferred_element_type=jnp.float32)
    sig = jax.nn.sigmoid(pre)
    updated = (rows.astype(jnp.float32) + pre * sig).astype(jnp.bfloat16)
    edge_in = jnp.where(
        edge_live[:, None], jnp.take(atoms_all, tgt_row, axis=0), jnp.zeros((), jnp.bfloat16)
    )
    edge_out = jnp.dot(edge_in, w_atom.T, preferred_element_type=jnp.float32)
    part_atom = jnp.dot(updated.T, edge_in, preferred_element_type=jnp.float32)
    pre_grad = (edge_out * sig * (1.0 + pre * (1.0 - sig))).astype(jnp.bfloat16)
    part_up = jnp.dot(aggregate.T, pre_grad, preferred_element_type=jnp.float32)
    aggregate_grad = jnp.dot(pre_grad, w_up.T, preferred_element_type=jnp.float32).astype(
        jnp.bfloat16
    )
    contrib = jnp.where(
        trip_live[:, None],
        jnp.take(aggregate_grad, local_dest, axis=0).astype(jnp.float32)
        * basis.astype(jnp.float32),
        jnp.float32(0.0),
    )
    partial_grad = jax.ops.segment_sum(
        contrib, source, num_segments=edge_slots * groups
    ).astype(jnp.bfloat16)
    blocks = partial_grad.reshape(groups, edge_slots, db)
    total = jnp.take(blocks, here, axis=0).astype(jnp.float32)
    for k in range(1, groups):
        piece = jnp.take(blocks, (here + k) % groups, axis=0)
        total = total + shifted(piece, "graph", groups, k).astype(jnp.float32)
    source_grad = total.astype(jnp.bfloat16)
    part_down = jnp.dot(rows.T, source_grad, preferred_element_type=jnp.float32)
    result = (edge_out + jnp.dot(source_grad, w_down.T, preferred_element_type=jnp.float32)).astype(
        jnp.bfloat16
    )

    width = da // groups
    atom_blocks = part_atom.reshape(de, groups, width)
    atom_sum = jnp.take(atom_blocks, here, axis=1)
    for k in range(1, groups):
        piece = jnp.take(atom_blocks, (here + k) % groups, axis=1)
        atom_sum = atom_sum + shifted(piece, "graph", groups, k)
    small = butterfly(jnp.concatenate([part_up.T, part_down], axis=1), "graph", groups)
    both = butterfly(jnp.concatenate([atom_sum, small], axis=1), "dp", dps)
    atom_grad = both[:, :width]
    up_grad = both[:, width : width + db].T
    down_grad = both[:, width + db :]
    return (result[None], atom_grad, up_grad, down_grad)


def solution(mesh):
    return jax.shard_map(
        local,
        mesh=mesh,
        in_specs=(
            P("dp", "graph", None),
            P("dp", "graph", None),
            P("dp", "graph", None),
            P("dp", "graph"),
            P("dp", "graph"),
            P("dp", "graph"),
            P("dp", "graph"),
            P("dp", "graph"),
            P("dp", "graph"),
            P(),
            P(),
            P(),
        ),
        out_specs=(P("dp", "graph", None), P(None, "graph"), P(), P()),
        check_vma=False,
    )
```

time: 703 us -> 462 us (0.66)
  waiting for transfers between devices: 472 us -> 116 us
  starting transfers between devices: 0.16 us -> 142 us
  other arithmetic: 162 us -> 76.2 us
  local copies, waits for them, and re-layouts: 22.2 us -> 90.3 us
  between operations: 15.2 us -> 2.92 us
    psum x1 -> x0, waiting for transfers between devices: 262 us -> none  [local(): lax.psum((part_atom, part_up, part_down), ('dp', 'graph'))]
    ppermute x0 -> x29, starting transfers between devices: none -> 142 us  [the longest x21 123 us: shifted(): return lax.ppermute(x, axis, [(i, (i + k) % size) for i in range(size)])]
    ppermute x0 -> x29, waiting for transfers between devices: none -> 116 us  [the longest x8 71.9 us: butterfly(): x = x + lax.ppermute(x, axis, [(i, i ^ bit) for i in range(size)])]
    all_gather x2 -> x0, waiting for transfers between devices: 115 us -> none  [the longest x1 61.5 us: local(): atoms_all = lax.all_gather(scaled, 'graph', axis=0, tiled=True)]
    reduce_scatter x1 -> x0, waiting for transfers between devices: 94.9 us -> none  [local(): lax.psum_scatter(partial_grad, 'graph', scatter_dimension=0, tiled=True)]
    scatter-add x2 -> x1, other arithmetic: 153 us -> 59 us  [local(): jax.ops.segment_sum(contrib, source, num_segments=edge_slots * groups)]
    another operation x0 -> x10, local copies, waits for them, and re-layouts: none -> 34.1 us  [the longest x9 33 us: local(): got = jnp.stack(pieces)]
    gather x1 -> x2, local copies, waits for them, and re-layouts: 9.4 us -> 29.5 us  [the longest x1 23.6 us: local(): feats = jnp.take(table, src_row, axis=0)]
  transfers between devices with their start and end apart: 4 -> 29, of which waited for: 4 -> 14; matrix products, arithmetic and copies ran while one was open for 5% -> 6% of each run, Pallas kernels for 0% -> 0%
where the time goes in v1:
time: 462 us; the launch traced here: 454 us
  starting transfers between devices  142 us (31%)
  waiting for transfers between devices  116 us (25%)
  local copies, waits for them, and re-layouts  90.3 us (20%)
  other arithmetic  76.2 us (16%)
  matrix products  25.9 us (6%)
    ppermute x21, starting transfers between devices, shifted(): return lax.ppermute(x, axis, [(i, (i + k) % size) for i in range(size)])  123 us
    ppermute x8, waiting for transfers between devices, butterfly(): x = x + lax.ppermute(x, axis, [(i, i ^ bit) for i in range(size)])  71.9 us
    scatter-add x1, other arithmetic, local(): jax.ops.segment_sum(contrib, source, num_segments=edge_slots * groups)  59 us
    ppermute x21, waiting for transfers between devices, shifted(): return lax.ppermute(x, axis, [(i, (i + k) % size) for i in range(size)])  44.3 us
    another operation x9, local copies, waits for them, and re-layouts, local(): got = jnp.stack(pieces)  33 us
    gather x1, local copies, waits for them, and re-layouts, local(): feats = jnp.take(table, src_row, axis=0)  23.6 us
    ppermute x8, starting transfers between devices, butterfly(): x = x + lax.ppermute(x, axis, [(i, i ^ bit) for i in range(size)])  19.6 us
    unnamed x70, local copies, waits for them, and re-layouts  14.3 us
  transfers between devices with their start and end apart: 29, of which 14 were waited for; matrix products, arithmetic and copies ran while one was open for 6% of the time, Pallas kernels for 0%

profile of v1, /device:TPU:5, one launch (start us, length us, event | category | flops | bytes accessed | tf_op | source)
XLA Modules:
  0.0 453.9 jit_solution(17403090487155087881)
XLA Ops:
  1.4 2.0 convolution_convert_fusion.1
  5.3 9.1 %collective-permute-start.5 = (bf16[196608]{0:T(1024)(128)(2,1)}, bf16[196608]{0:T(1024)(128)(2,1)S(1)}, u32[]{:S(2)}, u32[]{:S(2)}) collective-permute-start(bf16[196608]{0:T(1024)(128)(2,1)} %pad_maximum_fusion.1), channel_id=1, source_target_pairs={{0,6},{1,7},{2,0},{3,1},{4,2},{5,3},{6,4},{7,5},{8,14},{9,15},{10,... | collective-permute-start | bytes 1179656 | tf_op jit(solution)/shard_map/ppermute | solution.py:8
  14.4 6.3 %collective-permute-start.2 = (bf16[196608]{0:T(1024)(128)(2,1)}, bf16[196608]{0:T(1024)(128)(2,1)}, u32[]{:S(2)}, u32[]{:S(2)}) collective-permute-start(bf16[196608]{0:T(1024)(128)(2,1)} %pad_maximum_fusion.1), channel_id=1, source_target_pairs={{0,3},{1,4},{2,5},{3,6},{4,7},{5,0},{6,1},{7,2},{8,11},{9,12},{10,... | collective-permute-start | bytes 1179656 | tf_op jit(solution)/shard_map/ppermute | solution.py:8
  23.8 2.1 collective-permute-start.1
  25.9 13.7 %collective-permute-done.5 = bf16[196608]{0:T(1024)(128)(2,1)S(1)} collective-permute-done((bf16[196608]{0:T(1024)(128)(2,1)}, bf16[196608]{0:T(1024)(128)(2,1)S(1)}, u32[]{:S(2)}, u32[]{:S(2)}) %collective-permute-start.5) | collective-permute-done | bytes 393248 | tf_op jit(solution)/shard_map/ppermute | solution.py:8
  40.7 1.4 stack.27
  42.1 1.8 copy.80
  44.8 2.1 stack.34
  46.9 2.1 stack.33
  49.1 2.1 stack.32
  51.2 2.1 stack.31
  53.3 2.1 stack.30
  55.4 1.6 collective-permute-done.1
  57.0 2.1 stack.29
  59.1 2.1 stack.28
  61.3 16.8 %stack.35 = bf16[8,196608]{1,0:T(8,128)(2,1)} concatenate(bf16[1,196608]{1,0:T(2,128)(2,1)S(1)} %stack.27, bf16[1,196608]{1,0:T(2,128)(2,1)} %stack.28, bf16[1,196608]{1,0:T(2,128)(2,1)} %stack.29, bf16[1,196608]{1,0:T(2,128)(2,1)} %stack.30, bf16[1,196608]{1,0:T(2,128)(2,1)} %stack.31, bf16[1,196608]{1,0:T(2,128)(2,1)} %stack.32, bf16[1,196608]{1,0:T(2,128)(2,1)} %stack.33, ...), dimensions={0} | concatenate | bytes 6291456 | tf_op jit(solution)/shard_map/stack | solution.py:49
  78.0 3.8 fusion.60
  81.8 3.3 reshape.694
  85.1 5.1 %reshape.332 = bf16[12288,64]{1,0:T(8,128)(2,1)} reshape(bf16[786432]{0:T(1024)(128)(2,1)} %reshape.694) | data formatting | bytes 3145728 | tf_op jit(solution)/shard_map/reshape | solution.py:52
  90.2 23.6 %gather_fusion.1 = bf16[6144,64]{1,0:T(8,128)(2,1)} fusion(bf16[12288,64]{1,0:T(8,128)(2,1)} %reshape.332, s32[6144]{0:T(1024)S(1)} %broadcast_clamp_fusion.1), kind=kCustom, calls=%fused_computation.1 | custom fusion | bytes 1597440 | tf_op jit(solution)/shard_map/jit(_take)/gather | solution.py:56
  113.9 5.0 %fusion.11 = (bf16[6144,64]{1,0:T(8,128)(2,1)S(1)}, bf16[6144,64]{1,0:T(8,128)(2,1)S(1)}) fusion(bf16[1,6144,64]{2,1,0:T(8,128)(2,1)S(1)} %copy.80, bf16[6144,64]{1,0:T(8,128)(2,1)} %gather_fusion.1, pred[6144]{0:T(1024)(128)(4,1)S(1)} %copy-done.23), kind=kLoop, calls=%fused_computation.22 | loop fusion | flops 3145728 | bytes 3151872 | tf_op jit(solution)/shard_map/convert_element_type | solution.py:62
  118.9 10.0 %fusion.1 = f32[1536,128]{0,1:T(8,128)S(1)} fusion(s32[6144]{0:T(1024)S(1)} %bitcast.143, pred[6144]{0:T(1024)(128)(4,1)S(1)} %copy-done.21, bf16[6144,64]{1,0:T(8,128)(2,1)S(1)} %get-tuple-element.55, bf16[6144,64]{1,0:T(8,128)(2,1)S(1)} %get-tuple-element.54), kind=kOutput, calls=%fused_computation.6 | convolution fusion | flops 2437939200 | bytes 2390016 | tf_op jit(solution)/shard_map/dot_general | solution.py:65
  129.0 2.2 reshape.331
  131.3 5.9 %gather_fusion = bf16[1536,1024]{1,0:T(8,128)(2,1)} fusion(bf16[768,1024]{1,0:T(8,128)(2,1)S(1)} %reshape.331, s32[2048]{0:T(1024)S(1)} %copy-done.20), kind=kCustom, calls=%fused_computation | custom fusion | bytes 6297600 | tf_op jit(solution)/shard_map/jit(_take)/gather | solution.py:76
  137.1 4.3 fusion.58
  141.5 3.1 multiply_convert_fusion
  144.6 1.1 copy-done.5
  146.6 59.0 %scatter_custom_fusion = f32[12288,64]{1,0:T(8,128)} fusion(s32[6144]{0:T(1024)S(1)} %bitcast.141, f32[]{:T(128)} %constant.183.clone.1, bf16[1,6144,64]{2,1,0:T(8,128)(2,1)S(1)} %copy-done.3, pred[6144]{0:T(1024)(128)(4,1)S(1)} %copy-done.22, pred[6144]{0:T(1024)(128)(4,1)S(1)} %copy-done.21, bf16[]{:T(256)} %constant.181.clone.1, ...), kind=kCustom, calls=%fused_computation.13 | custom fusion | flops 2359296 | bytes 5150208 | tf_op jit(solution)/shard_map/scatter-add | solution.py:91
  205.6 3.0 convert_element_type.108
  208.6 1.1 constant_dynamic-slice_fusion.7
  209.8 0.9 copy.100
  210.8 1.9 copy.105
  212.7 1.8 copy.104
  215.4 0.9 copy.102
  216.7 46.1 %collective-permute-start.13 = (bf16[1536,64]{0,1:T(8,128)(2,1)S(1)}, bf16[1536,64]{0,1:T(8,128)(2,1)S(1)}, u32[]{:S(2)}, u32[]{:S(2)}) collective-permute-start(bf16[1536,64]{0,1:T(8,128)(2,1)S(1)} %select_bitcast_fusion.7), channel_id=1, source_target_pairs={{0,7},{1,0},{2,1},{3,2},{4,3},{5,4},{6,5},{7,6},{8,15},{9,8},{10,9... | collective-permute-start | bytes 589832 | tf_op jit(solution)/shard_map/ppermute | solution.py:8
  262.8 1.0 select_bitcast_fusion.12
  263.8 13.3 %collective-permute-start.8 = (bf16[1536,64]{0,1:T(8,128)(2,1)S(1)}, bf16[1536,64]{0,1:T(8,128)(2,1)S(1)}, u32[]{:S(2)}, u32[]{:S(2)}) collective-permute-start(bf16[1536,64]{0,1:T(8,128)(2,1)S(1)} %select_bitcast_fusion.12), channel_id=1, source_target_pairs={{0,2},{1,3},{2,4},{3,5},{4,6},{5,7},{6,0},{7,1},{8,10},{9,11},{10,... | collective-permute-start | bytes 589832 | tf_op jit(solution)/shard_map/ppermute | solution.py:8
  277.1 0.9 select_bitcast_fusion.11
  278.2 5.8 %collective-permute-start.10 = (bf16[1536,64]{0,1:T(8,128)(2,1)S(1)}, bf16[1536,64]{0,1:T(8,128)(2,1)S(1)}, u32[]{:S(2)}, u32[]{:S(2)}) collective-permute-start(bf16[1536,64]{0,1:T(8,128)(2,1)S(1)} %select_bitcast_fusion.10), channel_id=1, source_target_pairs={{0,4},{1,5},{2,6},{3,7},{4,0},{5,1},{6,2},{7,3},{8,12},{9,13},{10,... | collective-permute-start | bytes 589832 | tf_op jit(solution)/shard_map/ppermute | solution.py:8
  284.9 12.6 %collective-permute-start.12 = (bf16[1536,64]{0,1:T(8,128)(2,1)S(1)}, bf16[1536,64]{0,1:T(8,128)(2,1)S(1)}, u32[]{:S(2)}, u32[]{:S(2)}) collective-permute-start(bf16[1536,64]{0,1:T(8,128)(2,1)S(1)} %select_bitcast_fusion.8), channel_id=1, source_target_pairs={{0,6},{1,7},{2,0},{3,1},{4,2},{5,3},{6,4},{7,5},{8,14},{9,15},{10,... | collective-permute-start | bytes 589832 | tf_op jit(solution)/shard_map/ppermute | solution.py:8
  297.5 1.3 fusion.62
  298.8 5.4 %collective-permute-done.9 = bf16[1536,64]{0,1:T(8,128)(2,1)S(1)} collective-permute-done((bf16[1536,64]{0,1:T(8,128)(2,1)S(1)}, bf16[1536,64]{0,1:T(8,128)(2,1)S(1)}, u32[]{:S(2)}, u32[]{:S(2)}) %collective-permute-start.9) | collective-permute-done | bytes 196640 | tf_op jit(solution)/shard_map/ppermute | solution.py:8
  304.2 4.9 %collective-permute-done.10 = bf16[1536,64]{0,1:T(8,128)(2,1)S(1)} collective-permute-done((bf16[1536,64]{0,1:T(8,128)(2,1)S(1)}, bf16[1536,64]{0,1:T(8,128)(2,1)S(1)}, u32[]{:S(2)}, u32[]{:S(2)}) %collective-permute-start.10) | collective-permute-done | bytes 196640 | tf_op jit(solution)/shard_map/ppermute | solution.py:8
  309.1 4.2 collective-permute-done.11
  313.3 1.1 add_convert_fusion.2
  315.0 2.4 fusion.22
  317.7 1.5 collective-permute-start.14
  319.3 2.8 collective-permute-done.21
  322.1 5.4 %collective-permute-start.22 = (f32[512,128]{0,1:T(8,128)S(1)}, f32[512,128]{0,1:T(8,128)S(1)}, u32[]{:S(2)}, u32[]{:S(2)}) collective-permute-start(f32[512,128]{0,1:T(8,128)S(1)} %fusion.56), channel_id=1, source_target_pairs={{0,2},{1,3},{2,0},{3,1},{4,6},{5,7},{6,4},{7,5},{8,10},{9,11},{10,... | collective-permute-start | bytes 786440 | tf_op jit(solution)/shard_map/ppermute | solution.py:14
  327.6 5.3 %collective-permute-start.18 = (f32[512,128]{0,1:T(8,128)S(1)}, f32[512,128]{0,1:T(8,128)S(1)}, u32[]{:S(2)}, u32[]{:S(2)}) collective-permute-start(f32[512,128]{0,1:T(8,128)S(1)} %get-tuple-element.69), channel_id=1, source_target_pairs={{0,5},{1,6},{2,7},{3,0},{4,1},{5,2},{6,3},{7,4},{8,13},{9,14},{10,... | collective-permute-start | bytes 786440 | tf_op jit(solution)/shard_map/ppermute | solution.py:8
  333.5 4.8 %collective-permute-start.16 = (f32[512,128]{0,1:T(8,128)S(1)}, f32[512,128]{0,1:T(8,128)S(1)}, u32[]{:S(2)}, u32[]{:S(2)}) collective-permute-start(f32[512,128]{0,1:T(8,128)S(1)} %get-tuple-element.71), channel_id=1, source_target_pairs={{0,3},{1,4},{2,5},{3,6},{4,7},{5,0},{6,1},{7,2},{8,11},{9,12},{10,... | collective-permute-start | bytes 786440 | tf_op jit(solution)/shard_map/ppermute | solution.py:8
  338.3 13.6 %collective-permute-start.15 = (f32[512,128]{0,1:T(8,128)S(1)}, f32[512,128]{0,1:T(8,128)S(1)}, u32[]{:S(2)}, u32[]{:S(2)}) collective-permute-start(f32[512,128]{0,1:T(8,128)S(1)} %get-tuple-element.72), channel_id=1, source_target_pairs={{0,2},{1,3},{2,4},{3,5},{4,6},{5,7},{6,0},{7,1},{8,10},{9,11},{10,... | collective-permute-start | bytes 786440 | tf_op jit(solution)/shard_map/ppermute | solution.py:8
  351.9 8.0 %collective-permute-done.19 = f32[512,128]{0,1:T(8,128)S(1)} collective-permute-done((f32[512,128]{0,1:T(8,128)S(1)}, f32[512,128]{0,1:T(8,128)S(1)}, u32[]{:S(2)}, u32[]{:S(2)}) %collective-permute-start.19) | collective-permute-done | bytes 262176 | tf_op jit(solution)/shard_map/ppermute | solution.py:8
  359.9 8.2 %collective-permute-start.23 = (f32[512,128]{0,1:T(8,128)S(1)}, f32[512,128]{0,1:T(8,128)S(1)}, u32[]{:S(2)}, u32[]{:S(2)}) collective-permute-start(f32[512,128]{0,1:T(8,128)S(1)} %add.398), channel_id=1, source_target_pairs={{0,4},{1,5},{2,6},{3,7},{4,0},{5,1},{6,2},{7,3},{8,12},{9,13},{10,... | collective-permute-start | bytes 786440 | tf_op jit(solution)/shard_map/ppermute | solution.py:14
  368.2 6.5 %collective-permute-done.15 = f32[512,128]{0,1:T(8,128)S(1)} collective-permute-done((f32[512,128]{0,1:T(8,128)S(1)}, f32[512,128]{0,1:T(8,128)S(1)}, u32[]{:S(2)}, u32[]{:S(2)}) %collective-permute-start.15) | collective-permute-done | bytes 262176 | tf_op jit(solution)/shard_map/ppermute | solution.py:8
  374.9 8.9 %collective-permute-done.23 = f32[512,128]{0,1:T(8,128)S(1)} collective-permute-done((f32[512,128]{0,1:T(8,128)S(1)}, f32[512,128]{0,1:T(8,128)S(1)}, u32[]{:S(2)}, u32[]{:S(2)}) %collective-permute-start.23) | collective-permute-done | bytes 262176 | tf_op jit(solution)/shard_map/ppermute | solution.py:14
  384.7 1.5 collective-permute-done.24
  386.3 1.9 collective-permute-start.25
  388.2 11.8 %collective-permute-done.25 = f32[512,256]{0,1:T(8,128)S(1)} collective-permute-done((f32[512,256]{0,1:T(8,128)S(1)}, f32[512,256]{0,1:T(8,128)S(1)}, u32[]{:S(2)}, u32[]{:S(2)}) %collective-permute-start.25) | collective-permute-done | bytes 524320 | tf_op jit(solution)/shard_map/ppermute | solution.py:14
  400.1 3.0 collective-permute-start.26
  403.1 11.0 %collective-permute-done.26 = f32[512,256]{0,1:T(8,128)S(1)} collective-permute-done((f32[512,256]{0,1:T(8,128)S(1)}, f32[512,256]{0,1:T(8,128)S(1)}, u32[]{:S(2)}, u32[]{:S(2)}) %collective-permute-start.26) | collective-permute-done | bytes 524320 | tf_op jit(solution)/shard_map/ppermute | solution.py:14
  414.3 11.5 %collective-permute-done.27 = f32[512,256]{0,1:T(8,128)S(1)} collective-permute-done((f32[512,256]{0,1:T(8,128)S(1)}, f32[512,256]{0,1:T(8,128)S(1)}, u32[]{:S(2)}, u32[]{:S(2)}) %collective-permute-start.27) | collective-permute-done | bytes 524320 | tf_op jit(solution)/shard_map/ppermute | solution.py:14
  426.0 1.7 fusion.12
  427.8 24.2 %collective-permute-done.28 = f32[512,256]{0,1:T(8,128)S(1)} collective-permute-done((f32[512,256]{0,1:T(8,128)S(1)}, f32[512,256]{0,1:T(8,128)S(1)}, u32[]{:S(2)}, u32[]{:S(2)}) %collective-permute-start.28) | collective-permute-done | bytes 524320 | tf_op jit(solution)/shard_map/ppermute | solution.py:14
  (134 shorter events, 14.5 us)
Async XLA Ops:
  0.6 136.5 %copy-start = (bf16[512,1024]{1,0:T(8,128)(2,1)S(1)}, bf16[512,1024]{1,0:T(8,128)(2,1)}, u32[]{:S(2)}) copy-start(bf16[512,1024]{1,0:T(8,128)(2,1)} %param.27) | copy-start | bytes 3145732
  0.6 3.4 copy-start.17
  3.4 17.2 %copy-start.19 = (s32[1,1536]{1,0:T(1,128)S(1)}, s32[1,1536]{1,0:T(1,128)}, u32[]{:S(2)}) copy-start(s32[1,1536]{1,0:T(1,128)} %param.20) | copy-start | bytes 18436
  3.4 17.3 %copy-start.16 = (s32[1,6144]{1,0:T(1,128)S(1)}, s32[1,6144]{1,0:T(1,128)}, u32[]{:S(2)}) copy-start(s32[1,6144]{1,0:T(1,128)} %param.21) | copy-start | bytes 73732
  3.4 19.0 %copy-start.24 = (s32[1,6144]{1,0:T(1,128)S(1)}, s32[1,6144]{1,0:T(1,128)}, u32[]{:S(2)}) copy-start(s32[1,6144]{1,0:T(1,128)} %param.22) | copy-start | bytes 73732
  5.0 18.8 %collective-permute-start.6 = (bf16[196608]{0:T(1024)(128)(2,1)}, bf16[196608]{0:T(1024)(128)(2,1)S(1)}, u32[]{:S(2)}, u32[]{:S(2)}) collective-permute-start(bf16[196608]{0:T(1024)(128)(2,1)} %pad_maximum_fusion.1), channel_id=1, source_target_pairs={{0,7},{1,0},{2,1},{3,2},{4,3},{5,4},{6,5},{7,6},{8,15},{9,8},{10,9... | collective-permute-start | bytes 1179656 | tf_op jit(solution)/shard_map/ppermute | solution.py:8
  5.3 34.3 %collective-permute-start.5 = (bf16[196608]{0:T(1024)(128)(2,1)}, bf16[196608]{0:T(1024)(128)(2,1)S(1)}, u32[]{:S(2)}, u32[]{:S(2)}) collective-permute-start(bf16[196608]{0:T(1024)(128)(2,1)} %pad_maximum_fusion.1), channel_id=1, source_target_pairs={{0,6},{1,7},{2,0},{3,1},{4,2},{5,3},{6,4},{7,5},{8,14},{9,15},{10,... | collective-permute-start | bytes 1179656 | tf_op jit(solution)/shard_map/ppermute | solution.py:8
  14.4 34.7 %collective-permute-start.4 = (bf16[196608]{0:T(1024)(128)(2,1)}, bf16[196608]{0:T(1024)(128)(2,1)}, u32[]{:S(2)}, u32[]{:S(2)}) collective-permute-start(bf16[196608]{0:T(1024)(128)(2,1)} %pad_maximum_fusion.1), channel_id=1, source_target_pairs={{0,5},{1,6},{2,7},{3,0},{4,1},{5,2},{6,3},{7,4},{8,13},{9,14},{10,... | collective-permute-start | bytes 1179656 | tf_op jit(solution)/shard_map/ppermute | solution.py:8
  14.4 36.8 %collective-permute-start.3 = (bf16[196608]{0:T(1024)(128)(2,1)}, bf16[196608]{0:T(1024)(128)(2,1)}, u32[]{:S(2)}, u32[]{:S(2)}) collective-permute-start(bf16[196608]{0:T(1024)(128)(2,1)} %pad_maximum_fusion.1), channel_id=1, source_target_pairs={{0,4},{1,5},{2,6},{3,7},{4,0},{5,1},{6,2},{7,3},{8,12},{9,13},{10,... | collective-permute-start | bytes 1179656 | tf_op jit(solution)/shard_map/ppermute | solution.py:8
  14.4 38.9 %collective-permute-start.2 = (bf16[196608]{0:T(1024)(128)(2,1)}, bf16[196608]{0:T(1024)(128)(2,1)}, u32[]{:S(2)}, u32[]{:S(2)}) collective-permute-start(bf16[196608]{0:T(1024)(128)(2,1)} %pad_maximum_fusion.1), channel_id=1, source_target_pairs={{0,3},{1,4},{2,5},{3,6},{4,7},{5,0},{6,1},{7,2},{8,11},{9,12},{10,... | collective-permute-start | bytes 1179656 | tf_op jit(solution)/shard_map/ppermute | solution.py:8
  23.8 16.9 %copy-start.13 = (bf16[196608]{0:T(1024)(128)(2,1)}, bf16[196608]{0:T(1024)(128)(2,1)S(1)}, u32[]{:S(2)}) copy-start(bf16[196608]{0:T(1024)(128)(2,1)S(1)} %collective-permute-done.6) | copy-start | bytes 1179652
  23.8 33.2 %collective-permute-start.1 = (bf16[196608]{0:T(1024)(128)(2,1)}, bf16[196608]{0:T(1024)(128)(2,1)}, u32[]{:S(2)}, u32[]{:S(2)}) collective-permute-start(bf16[196608]{0:T(1024)(128)(2,1)} %pad_maximum_fusion.1), channel_id=1, source_target_pairs={{0,2},{1,3},{2,4},{3,5},{4,6},{5,7},{6,0},{7,1},{8,10},{9,11},{10,... | collective-permute-start | bytes 1179656 | tf_op jit(solution)/shard_map/ppermute | solution.py:8
  39.6 1.1 copy-start.14
  39.6 19.6 %collective-permute-start = (bf16[196608]{0:T(1024)(128)(2,1)}, bf16[196608]{0:T(1024)(128)(2,1)}, u32[]{:S(2)}, u32[]{:S(2)}) collective-permute-start(bf16[196608]{0:T(1024)(128)(2,1)} %pad_maximum_fusion.1), channel_id=1, source_target_pairs={{0,1},{1,2},{2,3},{3,4},{4,5},{5,6},{6,7},{7,0},{8,9},{9,10},{10,1... | collective-permute-start | bytes 1179656 | tf_op jit(solution)/shard_map/ppermute | solution.py:8
  43.9 70.0 %copy-start.2 = (bf16[1,6144,64]{2,1,0:T(8,128)(2,1)}, bf16[1,6144,64]{2,1,0:T(8,128)(2,1)S(1)}, u32[]{:S(2)}) copy-start(bf16[1,6144,64]{2,1,0:T(8,128)(2,1)S(1)} %copy.80) | copy-start | bytes 2359300
  90.2 23.6 %copy-start.23 = (pred[6144]{0:T(1024)(128)(4,1)S(1)}, pred[6144]{0:T(1024)(128)(4,1)}, u32[]{:S(2)}) copy-start(pred[6144]{0:T(1024)(128)(4,1)} %compare_and_fusion) | copy-start | bytes 18436
  113.9 5.0 %copy-start.21 = (pred[6144]{0:T(1024)(128)(4,1)S(1)}, pred[6144]{0:T(1024)(128)(4,1)}, u32[]{:S(2)}) copy-start(pred[6144]{0:T(1024)(128)(4,1)} %get-tuple-element.80) | copy-start | bytes 18436
  129.0 2.3 copy-start.20
  129.0 12.5 %copy-start.12 = (bf16[1536,64]{0,1:T(8,128)(2,1)}, bf16[1536,64]{0,1:T(8,128)(2,1)S(1)}, u32[]{:S(2)}) copy-start(bf16[1536,64]{0,1:T(8,128)(2,1)S(1)} %fusion.29) | copy-start | bytes 589828
  131.2 5.9 %copy-start.25 = (pred[1536]{0:T(1024)(128)(4,1)S(1)}, pred[1536]{0:T(1024)(128)(4,1)}, u32[]{:S(2)}) copy-start(pred[1536]{0:T(1024)(128)(4,1)} %get-tuple-element.78) | copy-start | bytes 4612
  131.2 5.9 %copy-start.26 = (pred[1536]{0:T(1024)(128)(4,1)S(1)}, pred[1536]{0:T(1024)(128)(4,1)}, u32[]{:S(2)}) copy-start(pred[1536]{0:T(1024)(128)(4,1)} %get-tuple-element.79) | copy-start | bytes 4612
  137.1 4.4 copy-start.18
  141.5 3.1 copy-start.7
  141.5 5.1 %copy-start.22 = (pred[6144]{0:T(1024)(128)(4,1)S(1)}, pred[6144]{0:T(1024)(128)(4,1)}, u32[]{:S(2)}) copy-start(pred[6144]{0:T(1024)(128)(4,1)} %get-tuple-element.81) | copy-start | bytes 18436
  144.6 1.1 copy-start.5
  144.6 2.0 copy-start.3
  210.8 86.7 %copy-start.6 = (bf16[1536,512]{1,0:T(8,128)(2,1)S(1)}, bf16[1536,512]{1,0:T(8,128)(2,1)}, u32[]{:S(2)}) copy-start(bf16[1536,512]{1,0:T(8,128)(2,1)} %copy-done.5) | copy-start | bytes 4718596
  215.4 62.7 %copy-start.11 = (bf16[1,1536,64]{1,2,0:T(8,128)(2,1)S(1)}, bf16[1,1536,64]{1,2,0:T(8,128)(2,1)}, u32[]{:S(2)}) copy-start(bf16[1,1536,64]{1,2,0:T(8,128)(2,1)} %copy.104) | copy-start | bytes 589828
  215.4 68.5 %copy-start.10 = (bf16[1,1536,64]{1,2,0:T(8,128)(2,1)S(1)}, bf16[1,1536,64]{1,2,0:T(8,128)(2,1)}, u32[]{:S(2)}) copy-start(bf16[1,1536,64]{1,2,0:T(8,128)(2,1)} %copy.105) | copy-start | bytes 589828
  216.6 97.9 %copy-start.4 = (bf16[1,1536,512]{2,1,0:T(8,128)(2,1)S(1)}, bf16[1,1536,512]{2,1,0:T(8,128)(2,1)}, u32[]{:S(2)}) copy-start(bf16[1,1536,512]{2,1,0:T(8,128)(2,1)} %param.16) | copy-start | bytes 4718596
  216.7 67.3 %collective-permute-start.13 = (bf16[1536,64]{0,1:T(8,128)(2,1)S(1)}, bf16[1536,64]{0,1:T(8,128)(2,1)S(1)}, u32[]{:S(2)}, u32[]{:S(2)}) collective-permute-start(bf16[1536,64]{0,1:T(8,128)(2,1)S(1)} %select_bitcast_fusion.7), channel_id=1, source_target_pairs={{0,7},{1,0},{2,1},{3,2},{4,3},{5,4},{6,5},{7,6},{8,15},{9,8},{10,9... | collective-permute-start | bytes 589832 | tf_op jit(solution)/shard_map/ppermute | solution.py:8
  262.7 22.1 %collective-permute-start.7 = (bf16[1536,64]{0,1:T(8,128)(2,1)S(1)}, bf16[1536,64]{0,1:T(8,128)(2,1)S(1)}, u32[]{:S(2)}, u32[]{:S(2)}) collective-permute-start(bf16[1536,64]{0,1:T(8,128)(2,1)S(1)} %select_bitcast_fusion.13), channel_id=1, source_target_pairs={{0,1},{1,2},{2,3},{3,4},{4,5},{5,6},{6,7},{7,0},{8,9},{9,10},{10,1... | collective-permute-start | bytes 589832 | tf_op jit(solution)/shard_map/ppermute | solution.py:8
  263.8 35.0 %collective-permute-start.8 = (bf16[1536,64]{0,1:T(8,128)(2,1)S(1)}, bf16[1536,64]{0,1:T(8,128)(2,1)S(1)}, u32[]{:S(2)}, u32[]{:S(2)}) collective-permute-start(bf16[1536,64]{0,1:T(8,128)(2,1)S(1)} %select_bitcast_fusion.12), channel_id=1, source_target_pairs={{0,2},{1,3},{2,4},{3,5},{4,6},{5,7},{6,0},{7,1},{8,10},{9,11},{10,... | collective-permute-start | bytes 589832 | tf_op jit(solution)/shard_map/ppermute | solution.py:8
  278.0 26.2 %collective-permute-start.9 = (bf16[1536,64]{0,1:T(8,128)(2,1)S(1)}, bf16[1536,64]{0,1:T(8,128)(2,1)S(1)}, u32[]{:S(2)}, u32[]{:S(2)}) collective-permute-start(bf16[1536,64]{0,1:T(8,128)(2,1)S(1)} %select_bitcast_fusion.11), channel_id=1, source_target_pairs={{0,3},{1,4},{2,5},{3,6},{4,7},{5,0},{6,1},{7,2},{8,11},{9,12},{10,... | collective-permute-start | bytes 589832 | tf_op jit(solution)/shard_map/ppermute | solution.py:8
  278.2 31.0 %collective-permute-start.10 = (bf16[1536,64]{0,1:T(8,128)(2,1)S(1)}, bf16[1536,64]{0,1:T(8,128)(2,1)S(1)}, u32[]{:S(2)}, u32[]{:S(2)}) collective-permute-start(bf16[1536,64]{0,1:T(8,128)(2,1)S(1)} %select_bitcast_fusion.10), channel_id=1, source_target_pairs={{0,4},{1,5},{2,6},{3,7},{4,0},{5,1},{6,2},{7,3},{8,12},{9,13},{10,... | collective-permute-start | bytes 589832 | tf_op jit(solution)/shard_map/ppermute | solution.py:8
  284.0 31.1 %copy-start.27 = (f32[1536,512]{1,0:T(8,128)S(1)}, f32[1536,512]{1,0:T(8,128)}, u32[]{:S(2)}) copy-start(f32[1536,512]{1,0:T(8,128)} %get-tuple-element.77) | copy-start | bytes 9437188
  284.0 31.0 %copy-start.9 = (bf16[1536,1024]{1,0:T(8,128)(2,1)S(1)}, bf16[1536,1024]{1,0:T(8,128)(2,1)}, u32[]{:S(2)}) copy-start(bf16[1536,1024]{1,0:T(8,128)(2,1)} %gather_fusion) | copy-start | bytes 9437188
  284.0 29.3 %collective-permute-start.11 = (bf16[1536,64]{0,1:T(8,128)(2,1)S(1)}, bf16[1536,64]{0,1:T(8,128)(2,1)S(1)}, u32[]{:S(2)}, u32[]{:S(2)}) collective-permute-start(bf16[1536,64]{0,1:T(8,128)(2,1)S(1)} %select_bitcast_fusion.9), channel_id=1, source_target_pairs={{0,5},{1,6},{2,7},{3,0},{4,1},{5,2},{6,3},{7,4},{8,13},{9,14},{10,... | collective-permute-start | bytes 589832 | tf_op jit(solution)/shard_map/ppermute | solution.py:8
  284.9 28.5 %collective-permute-start.12 = (bf16[1536,64]{0,1:T(8,128)(2,1)S(1)}, bf16[1536,64]{0,1:T(8,128)(2,1)S(1)}, u32[]{:S(2)}, u32[]{:S(2)}) collective-permute-start(bf16[1536,64]{0,1:T(8,128)(2,1)S(1)} %select_bitcast_fusion.8), channel_id=1, source_target_pairs={{0,6},{1,7},{2,0},{3,1},{4,2},{5,3},{6,4},{7,5},{8,14},{9,15},{10,... | collective-permute-start | bytes 589832 | tf_op jit(solution)/shard_map/ppermute | solution.py:8
  314.9 7.2 %collective-permute-start.21 = (f32[512,128]{0,1:T(8,128)S(1)}, f32[512,128]{0,1:T(8,128)S(1)}, u32[]{:S(2)}, u32[]{:S(2)}) collective-permute-start(f32[512,128]{0,1:T(8,128)S(1)} %pad_maximum_fusion.2), channel_id=1, source_target_pairs={{0,1},{1,0},{2,3},{3,2},{4,5},{5,4},{6,7},{7,6},{8,9},{9,8},{10,11... | collective-permute-start | bytes 786440 | tf_op jit(solution)/shard_map/ppermute | solution.py:14
  317.7 15.2 %collective-permute-start.14 = (f32[512,128]{0,1:T(8,128)S(1)}, f32[512,128]{0,1:T(8,128)S(1)}, u32[]{:S(2)}, u32[]{:S(2)}) collective-permute-start(f32[512,128]{0,1:T(8,128)S(1)} %get-tuple-element.66), channel_id=1, source_target_pairs={{0,1},{1,2},{2,3},{3,4},{4,5},{5,6},{6,7},{7,0},{8,9},{9,10},{10,1... | collective-permute-start | bytes 786440 | tf_op jit(solution)/shard_map/ppermute | solution.py:8
  319.2 14.3 %collective-permute-start.20 = (f32[512,128]{0,1:T(8,128)S(1)}, f32[512,128]{0,1:T(8,128)S(1)}, u32[]{:S(2)}, u32[]{:S(2)}) collective-permute-start(f32[512,128]{0,1:T(8,128)S(1)} %get-tuple-element.67), channel_id=1, source_target_pairs={{0,7},{1,0},{2,1},{3,2},{4,3},{5,4},{6,5},{7,6},{8,15},{9,8},{10,9... | collective-permute-start | bytes 786440 | tf_op jit(solution)/shard_map/ppermute | solution.py:8
  322.1 16.1 %collective-permute-start.22 = (f32[512,128]{0,1:T(8,128)S(1)}, f32[512,128]{0,1:T(8,128)S(1)}, u32[]{:S(2)}, u32[]{:S(2)}) collective-permute-start(f32[512,128]{0,1:T(8,128)S(1)} %fusion.56), channel_id=1, source_target_pairs={{0,2},{1,3},{2,0},{3,1},{4,6},{5,7},{6,4},{7,5},{8,10},{9,11},{10,... | collective-permute-start | bytes 786440 | tf_op jit(solution)/shard_map/ppermute | solution.py:14
  327.5 32.4 %collective-permute-start.19 = (f32[512,128]{0,1:T(8,128)S(1)}, f32[512,128]{0,1:T(8,128)S(1)}, u32[]{:S(2)}, u32[]{:S(2)}) collective-permute-start(f32[512,128]{0,1:T(8,128)S(1)} %get-tuple-element.68), channel_id=1, source_target_pairs={{0,6},{1,7},{2,0},{3,1},{4,2},{5,3},{6,4},{7,5},{8,14},{9,15},{10,... | collective-permute-start | bytes 786440 | tf_op jit(solution)/shard_map/ppermute | solution.py:8
  327.6 40.6 %collective-permute-start.18 = (f32[512,128]{0,1:T(8,128)S(1)}, f32[512,128]{0,1:T(8,128)S(1)}, u32[]{:S(2)}, u32[]{:S(2)}) collective-permute-start(f32[512,128]{0,1:T(8,128)S(1)} %get-tuple-element.69), channel_id=1, source_target_pairs={{0,5},{1,6},{2,7},{3,0},{4,1},{5,2},{6,3},{7,4},{8,13},{9,14},{10,... | collective-permute-start | bytes 786440 | tf_op jit(solution)/shard_map/ppermute | solution.py:8
  332.9 35.3 %collective-permute-start.17 = (f32[512,128]{0,1:T(8,128)S(1)}, f32[512,128]{0,1:T(8,128)S(1)}, u32[]{:S(2)}, u32[]{:S(2)}) collective-permute-start(f32[512,128]{0,1:T(8,128)S(1)} %get-tuple-element.70), channel_id=1, source_target_pairs={{0,4},{1,5},{2,6},{3,7},{4,0},{5,1},{6,2},{7,3},{8,12},{9,13},{10,... | collective-permute-start | bytes 786440 | tf_op jit(solution)/shard_map/ppermute | solution.py:8
  333.5 34.7 %collective-permute-start.16 = (f32[512,128]{0,1:T(8,128)S(1)}, f32[512,128]{0,1:T(8,128)S(1)}, u32[]{:S(2)}, u32[]{:S(2)}) collective-permute-start(f32[512,128]{0,1:T(8,128)S(1)} %get-tuple-element.71), channel_id=1, source_target_pairs={{0,3},{1,4},{2,5},{3,6},{4,7},{5,0},{6,1},{7,2},{8,11},{9,12},{10,... | collective-permute-start | bytes 786440 | tf_op jit(solution)/shard_map/ppermute | solution.py:8
  338.3 36.4 %collective-permute-start.15 = (f32[512,128]{0,1:T(8,128)S(1)}, f32[512,128]{0,1:T(8,128)S(1)}, u32[]{:S(2)}, u32[]{:S(2)}) collective-permute-start(f32[512,128]{0,1:T(8,128)S(1)} %get-tuple-element.72), channel_id=1, source_target_pairs={{0,2},{1,3},{2,4},{3,5},{4,6},{5,7},{6,0},{7,1},{8,10},{9,11},{10,... | collective-permute-start | bytes 786440 | tf_op jit(solution)/shard_map/ppermute | solution.py:8
  359.9 23.9 %collective-permute-start.23 = (f32[512,128]{0,1:T(8,128)S(1)}, f32[512,128]{0,1:T(8,128)S(1)}, u32[]{:S(2)}, u32[]{:S(2)}) collective-permute-start(f32[512,128]{0,1:T(8,128)S(1)} %add.398), channel_id=1, source_target_pairs={{0,4},{1,5},{2,6},{3,7},{4,0},{5,1},{6,2},{7,3},{8,12},{9,13},{10,... | collective-permute-start | bytes 786440 | tf_op jit(solution)/shard_map/ppermute | solution.py:14
  383.9 42.1 %copy-start.8 = (f32[1536,512]{1,0:T(8,128)S(1)}, f32[1536,512]{1,0:T(8,128)}, u32[]{:S(2)}) copy-start(f32[1536,512]{1,0:T(8,128)} %copy-done.7) | copy-start | bytes 9437188
  383.9 42.1 %copy-start.15 = (bf16[512,64]{0,1:T(8,128)(2,1)S(1)}, bf16[512,64]{0,1:T(8,128)(2,1)}, u32[]{:S(2)}) copy-start(bf16[512,64]{0,1:T(8,128)(2,1)} %param.25) | copy-start | bytes 196612
  383.9 2.3 collective-permute-start.24
  386.3 13.7 %collective-permute-start.25 = (f32[512,256]{0,1:T(8,128)S(1)}, f32[512,256]{0,1:T(8,128)S(1)}, u32[]{:S(2)}, u32[]{:S(2)}) collective-permute-start(f32[512,256]{0,1:T(8,128)S(1)} %fusion.57), channel_id=1, source_target_pairs={{0,16},{8,24},{16,0},{24,8},{32,48},{40,56},{48,32},{56,40},{64,80... | collective-permute-start | bytes 1572872 | tf_op jit(solution)/shard_map/ppermute | solution.py:14
  400.1 14.0 %collective-permute-start.26 = (f32[512,256]{0,1:T(8,128)S(1)}, f32[512,256]{0,1:T(8,128)S(1)}, u32[]{:S(2)}, u32[]{:S(2)}) collective-permute-start(f32[512,256]{0,1:T(8,128)S(1)} %add.401), channel_id=1, source_target_pairs={{0,32},{8,40},{16,48},{24,56},{32,0},{40,8},{48,16},{56,24},{64,96... | collective-permute-start | bytes 1572872 | tf_op jit(solution)/shard_map/ppermute | solution.py:14
  414.2 11.6 %collective-permute-start.27 = (f32[512,256]{0,1:T(8,128)S(1)}, f32[512,256]{0,1:T(8,128)S(1)}, u32[]{:S(2)}, u32[]{:S(2)}) collective-permute-start(f32[512,256]{0,1:T(8,128)S(1)} %add.402), channel_id=1, source_target_pairs={{0,64},{8,72},{16,80},{24,88},{32,96},{40,104},{48,112},{56,120},{... | collective-permute-start | bytes 1572872 | tf_op jit(solution)/shard_map/ppermute | solution.py:14
  425.8 27.8 %copy-start.1 = (bf16[512,1024]{1,0:T(8,128)(2,1)S(1)}, bf16[512,1024]{1,0:T(8,128)(2,1)}, u32[]{:S(2)}) copy-start(bf16[512,1024]{1,0:T(8,128)(2,1)} %param.27) | copy-start | bytes 3145732
  425.9 26.1 %collective-permute-start.28 = (f32[512,256]{0,1:T(8,128)S(1)}, f32[512,256]{0,1:T(8,128)S(1)}, u32[]{:S(2)}, u32[]{:S(2)}) collective-permute-start(f32[512,256]{0,1:T(8,128)S(1)} %add.403), channel_id=1, source_target_pairs={{0,128},{8,136},{16,144},{24,152},{32,160},{40,168},{48,176},{56,1... | collective-permute-start | bytes 1572872 | tf_op jit(solution)/shard_map/ppermute | solution.py:14
